TPU v7x, 512 devices: a whole 4x8x8 slice. The times are simulated.
512 devices in a mesh: seq: 64 (over z, x, core), head: 8 (over y).
Axes of the slice: x: 4, y: 8, z: 8, core: 2. Of those that a mesh axis runs over, the one named last changes fastest.
Arguments:
- projected: float32 [65536, 2560], P(('seq', 'head')), may hold values from -6 to 6
- out_grads: float32 [65536, 2048], P(('seq', 'head')), may hold values from -6 to 6
- conv_weight: float32 [3, 2560], replicated, may hold values from -2.4 to 2.4
- doc_lengths: int32 [16], replicated, may hold values from 1 to 32768, 65536 in all
Outputs:
- grad_projected: float32 [65536, 2560], P(('seq', 'head'))
- grad_conv: float32 [3, 2560], replicated
Inputs may be any that keep to these rules, and one draw needn't show every extreme that they name: `doc_lengths`: the 16 documents fill the 65536 tokens end to end; the longest holds exactly half of 65536 tokens.
All inputs are finite; a program needn't handle non-finite values.
Results may differ from a plain program's by a relative error of at most 0.0003.
Values sent between devices are 32-bit elements; how exact they have to be, the bound alone decides.
No kernel may reach another device: no remote copies, remote signals or barrier semaphores. Data moves between devices by JAX's collectives and lax.ppermute only.
A program may use at most 128 MiB of HBM per device.

v0:
```python
import math
import jax
import jax.numpy as jnp
import numpy as np
from jax import lax
from jax.sharding import PartitionSpec as P

KEY_DIM = 16
HEAD_DIM = 128
HIGHEST = lax.Precision.HIGHEST


def carried_in(x, axis, combine, identity, reverse):
    length, here = (lax.axis_size(axis), lax.axis_index(axis))
    everything = jax.tree.map(lambda part: lax.all_gather(part, axis), x)
    start = jax.tree.map(
        lambda part, zero: jnp.broadcast_to(jnp.asarray(zero, part.dtype), part.shape), x, identity
    )

    def lap(k, before):
        at = length - 1 - k if reverse else k
        reached = at > here if reverse else at < here
        new = combine(before, jax.tree.map(lambda part: part[at], everything))
        return jax.tree.map(lambda a, b: jnp.where(reached, a, b), new, before)

    return lax.fori_loop(0, length, lap, start)


def passed_along(value, axis, steps):
    count = lax.axis_size(axis)
    initial, last = (max(0, -steps), min(count, count - steps))
    return lax.ppermute(value, axis, [(source, source + steps) for source in range(initial, last)])


def feature_map(columns):
    key_size = columns.shape[1]
    upper_i, upper_j = np.triu_indices(key_size)
    factors = np.where(upper_i == upper_j, 1.0 / math.sqrt(2.0), 1.0).astype(np.float32)
    products = columns[:, upper_i, :] * columns[:, upper_j, :] * jnp.asarray(factors)[None, :, None]
    constant = jnp.ones((columns.shape[0], 1, columns.shape[2]), jnp.float32)
    return jnp.concatenate([constant, columns, products], axis=1)


def doc_place(doc_lengths, anchor, amount):
    positions = anchor + jnp.arange(amount, dtype=jnp.int32)
    starts = jnp.cumsum(doc_lengths) - doc_lengths
    begins = jnp.max(jnp.where(starts[None, :] <= positions[:, None], starts[None, :], 0), axis=1)
    return (begins, positions - begins)


def conv_forward(signal, leading, weights, offsets):
    row_count = signal.shape[0]
    behind = jnp.concatenate([leading, signal], axis=0)
    back_one = behind[1 : row_count + 1] * (offsets[0:row_count] >= 1).astype(jnp.float32)[:, None]
    back_two = behind[0:row_count] * (offsets[0:row_count] >= 2).astype(jnp.float32)[:, None]
    return weights[0] * signal + weights[1] * back_one + weights[2] * back_two


def conv_backward(grad_rows, trailing, signal, leading, weights, offsets):
    row_count = grad_rows.shape[0]
    ahead_rows = jnp.concatenate([grad_rows, trailing], axis=0)
    ahead_one = (
        ahead_rows[1 : row_count + 1]
        * (offsets[1 : row_count + 1] >= 1).astype(jnp.float32)[:, None]
    )
    ahead_two = (
        ahead_rows[2 : row_count + 2]
        * (offsets[2 : row_count + 2] >= 2).astype(jnp.float32)[:, None]
    )
    grad_signal = weights[0] * grad_rows + weights[1] * ahead_one + weights[2] * ahead_two
    behind = jnp.concatenate([leading, signal], axis=0)
    own_one = (offsets[0:row_count] >= 1).astype(jnp.float32)[:, None]
    own_two = (offsets[0:row_count] >= 2).astype(jnp.float32)[:, None]
    grad_weights = jnp.stack(
        [
            jnp.sum(grad_rows * signal, axis=0),
            jnp.sum(grad_rows * behind[1 : row_count + 1] * own_one, axis=0),
            jnp.sum(grad_rows * behind[0:row_count] * own_two, axis=0),
        ],
        axis=0,
    )
    return (grad_signal, grad_weights)


def combine(earlier, following):
    carry_keep = 1.0 - following[2]
    return (
        following[0] + carry_keep[:, None, None] * earlier[0],
        following[1] + carry_keep[:, None] * earlier[1],
        jnp.maximum(earlier[2], following[2]),
    )


def attention_grads(mixed_rows, out_flat, begins, stretch_start):
    length = mixed_rows.shape[0]
    head_width = 2 * KEY_DIM + HEAD_DIM
    local_heads = mixed_rows.shape[1] // head_width
    block_len = min(128, length)
    blocks = length // block_len
    scale_key = KEY_DIM ** (-0.25)
    shaped = mixed_rows.reshape(length, local_heads, head_width)
    query_cols = jnp.transpose(shaped[:, :, :KEY_DIM], (1, 2, 0)) * scale_key
    key_cols = jnp.transpose(shaped[:, :, KEY_DIM : 2 * KEY_DIM], (1, 2, 0)) * scale_key
    values = shaped[:, :, 2 * KEY_DIM :]
    upstream = out_flat.reshape(length, local_heads, HEAD_DIM)
    query_feat, query_pull = jax.vjp(feature_map, query_cols)
    key_feat, key_pull = jax.vjp(feature_map, key_cols)
    feat_count = query_feat.shape[1]
    last_begin = begins[length - 1]
    has_start = (last_begin >= stretch_start).astype(jnp.float32).reshape(1)
    tail_mask = (begins == last_begin).astype(jnp.float32)
    tail_feat = key_feat * tail_mask[None, None, :]
    tail_state = jnp.einsum("hfl,lhe->hfe", tail_feat, values, precision=HIGHEST)
    tail_norm = jnp.sum(tail_feat, axis=2)
    identity = (jnp.zeros_like(tail_state), jnp.zeros_like(tail_norm), jnp.zeros((1,), jnp.float32))
    prefix = carried_in((tail_state, tail_norm, has_start), "seq", combine, identity, False)
    causal = jnp.arange(block_len)[:, None] >= jnp.arange(block_len)[None, :]
    indices = jnp.arange(blocks, dtype=jnp.int32)

    def forward_block(carried, block_index):
        carry_state, carry_norm = carried
        offset_rows = block_index * block_len
        block_start = stretch_start + offset_rows
        query_blk = lax.dynamic_slice_in_dim(query_feat, offset_rows, block_len, 2)
        key_blk = lax.dynamic_slice_in_dim(key_feat, offset_rows, block_len, 2)
        value_blk = lax.dynamic_slice_in_dim(values, offset_rows, block_len, 0)
        doc_blk = lax.dynamic_slice_in_dim(begins, offset_rows, block_len, 0)
        allowed = causal & (doc_blk[:, None] == doc_blk[None, :])
        scores = jnp.where(
            allowed[None], jnp.einsum("hft,hfs->hts", query_blk, key_blk, precision=HIGHEST), 0.0
        )
        from_carry = (doc_blk < block_start).astype(jnp.float32)
        numerator = jnp.einsum("hts,she->the", scores, value_blk, precision=HIGHEST) + from_carry[
            :, None, None
        ] * jnp.einsum("hft,hfe->the", query_blk, carry_state, precision=HIGHEST)
        denominator = jnp.sum(scores, axis=2) + from_carry[None, :] * jnp.einsum(
            "hft,hf->ht", query_blk, carry_norm, precision=HIGHEST
        )
        block_tail = (doc_blk == doc_blk[block_len - 1]).astype(jnp.float32)
        carry_keep = (doc_blk[block_len - 1] < block_start).astype(jnp.float32)
        tail_keys = key_blk * block_tail[None, None, :]
        next_state = (
            jnp.einsum("hfs,she->hfe", tail_keys, value_blk, precision=HIGHEST)
            + carry_keep * carry_state
        )
        next_norm = jnp.sum(tail_keys, axis=2) + carry_keep * carry_norm
        return ((next_state, next_norm), (numerator, denominator, carry_state, carry_norm, scores))

    forward_out = lax.scan(forward_block, (prefix[0], prefix[1]), indices)
    numerators, denominators, states, norms, kept_scores = forward_out[1]
    denom_rows = jnp.transpose(denominators, (0, 2, 1)).reshape(length, local_heads)
    attended = numerators.reshape(length, local_heads, HEAD_DIM) / denom_rows[:, :, None]
    grad_num = upstream / denom_rows[:, :, None]
    scalar_grad = -jnp.sum(upstream * attended, axis=2) / denom_rows
    lead_mask = (begins < stretch_start).astype(jnp.float32)
    lead_feat = query_feat * lead_mask[None, None, :]
    lead_state = jnp.einsum("hfl,lhe->hfe", lead_feat, grad_num, precision=HIGHEST)
    lead_norm = jnp.einsum("hfl,lh->hf", lead_feat, scalar_grad, precision=HIGHEST)
    suffix = carried_in((lead_state, lead_norm, has_start), "seq", combine, identity, True)

    def backward_block(carried, inputs):
        back_state, back_norm = carried
        block_index, carry_state, carry_norm, scores = inputs
        offset_rows = block_index * block_len
        block_start = stretch_start + offset_rows
        query_blk = lax.dynamic_slice_in_dim(query_feat, offset_rows, block_len, 2)
        key_blk = lax.dynamic_slice_in_dim(key_feat, offset_rows, block_len, 2)
        value_blk = lax.dynamic_slice_in_dim(values, offset_rows, block_len, 0)
        doc_blk = lax.dynamic_slice_in_dim(begins, offset_rows, block_len, 0)
        grad_blk = lax.dynamic_slice_in_dim(grad_num, offset_rows, block_len, 0)
        scalar_blk = lax.dynamic_slice_in_dim(scalar_grad, offset_rows, block_len, 0)
        scalar_cols = scalar_blk.T
        allowed = causal & (doc_blk[:, None] == doc_blk[None, :])
        dscores = jnp.where(
            allowed[None],
            jnp.einsum("the,she->hts", grad_blk, value_blk, precision=HIGHEST)
            + scalar_cols[:, :, None],
            0.0,
        )
        from_carry = (doc_blk < block_start).astype(jnp.float32)
        block_tail = (doc_blk == doc_blk[block_len - 1]).astype(jnp.float32)
        carry_keep = (doc_blk[block_len - 1] < block_start).astype(jnp.float32)
        grad_query = jnp.einsum("hts,hfs->hft", dscores, key_blk, precision=HIGHEST) + from_carry[
            None, None, :
        ] * (
            jnp.einsum("hfe,the->hft", carry_state, grad_blk, precision=HIGHEST)
            + carry_norm[:, :, None] * scalar_cols[:, None, :]
        )
        grad_key = jnp.einsum("hts,hft->hfs", dscores, query_blk, precision=HIGHEST) + block_tail[
            None, None, :
        ] * (
            jnp.einsum("hfe,she->hfs", back_state, value_blk, precision=HIGHEST)
            + back_norm[:, :, None]
        )
        grad_value = jnp.einsum("hts,the->she", scores, grad_blk, precision=HIGHEST) + block_tail[
            :, None, None
        ] * jnp.einsum("hfs,hfe->she", key_blk, back_state, precision=HIGHEST)
        lead_blk = query_blk * from_carry[None, None, :]
        next_state = (
            jnp.einsum("hft,the->hfe", lead_blk, grad_blk, precision=HIGHEST)
            + carry_keep * back_state
        )
        next_norm = (
            jnp.einsum("hft,th->hf", lead_blk, scalar_blk, precision=HIGHEST)
            + carry_keep * back_norm
        )
        return ((next_state, next_norm), (grad_query, grad_key, grad_value))

    swept_back = lax.scan(
        backward_block, (suffix[0], suffix[1]), (indices, states, norms, kept_scores), reverse=True
    )
    grad_qblocks, grad_kblocks, grad_vblocks = swept_back[1]
    query_grad = jnp.transpose(grad_qblocks, (1, 2, 0, 3)).reshape(local_heads, feat_count, length)
    key_grad = jnp.transpose(grad_kblocks, (1, 2, 0, 3)).reshape(local_heads, feat_count, length)
    value_grad = grad_vblocks.reshape(length, local_heads, HEAD_DIM)
    query_in = jnp.transpose(query_pull(query_grad)[0] * scale_key, (2, 0, 1))
    key_in = jnp.transpose(key_pull(key_grad)[0] * scale_key, (2, 0, 1))
    return jnp.concatenate([query_in, key_in, value_grad], axis=2).reshape(
        length, local_heads * head_width
    )


def on_device(projected, out_grads, conv_weight, doc_lengths):
    row_count = projected.shape[0]
    head_count = lax.axis_size("head")
    seq_index = lax.axis_index("seq")
    head_index = lax.axis_index("head")
    group_len = row_count * head_count
    token_base = (seq_index * head_count + head_index) * row_count
    stretch_start = seq_index * group_len
    token_begins, token_offsets = doc_place(doc_lengths, token_base, row_count + 2)
    leading = passed_along(projected[row_count - 2 :], ("seq", "head"), 1)
    outgoing = conv_forward(projected, leading, conv_weight, token_offsets)
    arrived, upstream = (
        lax.all_to_all(outgoing, "head", split_axis=1, concat_axis=0, tiled=True),
        lax.all_to_all(out_grads, "head", split_axis=1, concat_axis=0, tiled=True),
    )
    group_begins, group_offsets = doc_place(doc_lengths, stretch_start, group_len + 2)
    grad_mixed = attention_grads(arrived, upstream, group_begins[:group_len], stretch_start)
    returned = lax.all_to_all(grad_mixed, "head", split_axis=0, concat_axis=1, tiled=True)
    trailing = passed_along(returned[:2], ("seq", "head"), -1)
    grad_projected, weight_part = conv_backward(
        returned, trailing, projected, leading, conv_weight, token_offsets
    )
    grad_conv = lax.psum(weight_part, ("seq", "head"))
    return (grad_projected, grad_conv)


def solution(mesh):
    return jax.shard_map(
        on_device,
        mesh=mesh,
        in_specs=(P(("seq", "head"), None), P(("seq", "head"), None), P(), P()),
        out_specs=(P(("seq", "head"), None), P()),
        check_vma=False,
    )
```

profile of v0, /device:TPU:1, one launch (start us, length us, event | category | flops | bytes accessed | tf_op | source)
XLA Modules:
  0.0 1203.6 jit_solution(1783652886522364890)
XLA Ops:
  20.8 6.1 all-to-all-start
  28.4 33.2 %all-to-all-done = f32[128,8,320]{0,2,1:T(8,128)S(1)} async-done(((f32[128,8,320]{0,2,1:T(8,128)}), f32[128,8,320]{0,2,1:T(8,128)S(1)}, u32[]{:S(2)}, u32[]{:S(2)}) %all-to-all-start) | async-done | bytes 1310752 | tf_op jit(solution)/shard_map/all_to_all | solution.py:235
  76.8 4.8 broadcast_multiply_fusion.1
  91.7 131.3 %all-reduce = f32[64]{0:T(128)S(1)} all-reduce(f32[64]{0:T(128)S(1)} %dynamic-update-slice), channel_id=1, replica_groups=mesh['seq'=64,'head'=8] {'seq'}, use_global_device_ids=true, to_apply=%add | all-reduce | flops 64 | bytes 512
  232.5 51.4 %all-gather.4 = f32[64,2,153]{2,1,0:T(2,128)S(1)} all-gather(f32[1,2,153]{2,1,0:T(2,128)S(1)} %copy.127), channel_id=3, replica_groups=mesh['seq'=64,'head'=8] {'seq'}, dimensions={0}, use_global_device_ids=true | all-gather | bytes 79560 | tf_op jit(solution)/shard_map/all_gather | solution.py:15
  283.9 187.7 %while.82 = (s32[]{:T(128)}, f32[2,153,128]{2,1,0:T(8,128)S(1)}, f32[2,153]{1,0:T(2,128)S(1)}, s32[]{:T(128)}, f32[64,2,153,128]{3,2,1,0:T(8,128)}, /*index=5*/f...) while((s32[]{:T(128)}, f32[2,153,128]{2,1,0:T(8,128)S(1)}, ...), condition=%wide.region_5.6_spmd.clone, body=%wide.region_4.5_spmd.clone.sunk | while | flops 157901 | bytes 473831 | solution.py:26
  472.9 110.3 %while.80 = (s32[]{:T(128)}, f32[2,153,128]{2,1,0:T(8,128)S(1)}, f32[2,153]{1,0:T(2,128)S(1)}, f32[8,128,2,128]{1,0,3,2:T(8,128)}, f32[8,2,128]{2,1,0:T(2,128)S(...) while((s32[]{:T(128)}, f32[2,153,128]{2,1,0:T(8,128)S(1)}, ...), condition=%wide.region_9.10_spmd.clone, body=%wide.region_6.9_spmd.clone.sunk | while | flops 231664960 | bytes 3280461 | solution.py:149
  490.7 4.8 dynamic_update_slice.74
  504.5 4.8 dynamic_update_slice.74
  518.3 4.8 dynamic_update_slice.74
  532.1 4.8 dynamic_update_slice.74
  545.9 4.8 dynamic_update_slice.74
  573.4 4.8 dynamic_update_slice.74
  593.5 49.5 %all-gather.5 = f32[64,2,153]{2,1,0:T(2,128)S(1)} all-gather(f32[1,2,153]{2,1,0:T(2,128)S(1)} %bitcast.282), channel_id=5, replica_groups=mesh['seq'=64,'head'=8] {'seq'}, dimensions={0}, use_global_device_ids=true | all-gather | bytes 79560 | tf_op jit(solution)/shard_map/all_gather | solution.py:15
  643.0 36.5 %all-gather.11.cloned.1.call-done = f32[128,153,128]{2,1,0:T(8,128)} async-done(((f32[2,153,128]{2,1,0:T(8,128)}), f32[128,153,128]{2,1,0:T(8,128)}) %all-gather.11.cloned.1.call-update) | async-done | bytes 10027024 | tf_op jit(solution)/shard_map/all_gather | solution.py:15
  679.5 195.2 %while.83 = (s32[]{:T(128)}, f32[2,153,128]{2,1,0:T(8,128)S(1)}, f32[2,153]{1,0:T(2,128)S(1)}, s32[]{:T(128)}, f32[64,2,153,128]{3,2,1,0:T(8,128)}, /*index=5*/f...) while((s32[]{:T(128)}, f32[2,153,128]{2,1,0:T(8,128)S(1)}, ...), condition=%wide.region_12.13_spmd.clone, body=%wide.region_11.12_spmd.clone.sunk | while | flops 157905 | bytes 473893 | solution.py:26
  878.2 112.1 %while.81 = (s32[]{:T(128)}, f32[2,153,128]{2,1,0:T(8,128)S(1)}, f32[2,153]{1,0:T(2,128)S(1)}, f32[8,2,153,128]{3,2,1,0:T(8,128)}, f32[8,2,153,128]{3,2,1,0:T(8,...) while((s32[]{:T(128)}, f32[2,153,128]{2,1,0:T(8,128)S(1)}, ...), condition=%wide.region_14.15_spmd.clone, body=%wide.region_13.14_spmd.clone.sunk | while | flops 462717824 | bytes 4866477 | solution.py:209
  998.9 5.9 fusion.90
  1004.9 14.0 %scatter_fusion = f32[2,16,1024]{2,0,1:T(2,128)S(1)} fusion(f32[2,16,1024]{2,0,1:T(2,128)S(1)} %split.16, s32[136]{0:T(256)S(1)} %copy-done.23, f32[136,2,1024]{2,1,0:T(2,128)} %get-tuple-element.1103), kind=kCustom, calls=%fused_computation.4 | custom fusion | flops 278528 | bytes 3342880 | tf_op jit(solution)/shard_map/transpose(jvp())/scatter-add | solution.py:39
  1018.9 7.6 scatter_fusion.1
  1027.7 7.6 scatter_fusion.3
  1035.3 7.6 scatter_fusion.2
  1048.3 40.7 %all_to_all.51 = f32[8,128,320]{1,2,0:T(8,128)S(1)} all-to-all(f32[8,128,320]{1,2,0:T(8,128)S(1)} %copy.143), channel_id=1, replica_groups=mesh['seq'=64,'head'=8] {'head'}, dimensions={0} | all-to-all | bytes 2621440 | tf_op jit(solution)/shard_map/all_to_all | solution.py:240
  1093.7 95.5 %psum.7 = f32[3,2560]{1,0:T(4,128)} all-reduce(f32[3,2560]{1,0:T(4,128)S(1)} %pad_maximum_fusion.5), channel_id=1, replica_groups=mesh['seq'=64,'head'=8] {'seq','head'}, use_global_device_ids=true, to_apply=%region_22.23 | all-reduce | flops 7680 | bytes 61440 | tf_op jit(solution)/shard_map/psum | solution.py:245
  (838 shorter events, 642.5 us)
Async XLA Ops:
  8.1 9.1 collective-permute-start
  17.2 3.6 copy-start.3
  20.8 6.9 copy-start.24
  20.8 6.9 copy-start.23
  20.8 40.9 %all-to-all-start = ((f32[128,8,320]{0,2,1:T(8,128)}), f32[128,8,320]{0,2,1:T(8,128)S(1)}, u32[]{:S(2)}, u32[]{:S(2)}) async-start(f32[128,8,320]{0,2,1:T(8,128)} %bitcast.265), calls=%async_computation | async-start | bytes 2621440 | tf_op jit(solution)/shard_map/all_to_all | solution.py:235
  26.9 257.1 %all-gather.9.cloned.1.call-start = ((), (), s32[]{:S(2)}) async-start(), calls=%async_computation.3 | async-start | bytes 10649600 | tf_op jit(solution)/shard_map/all_gather | solution.py:15
  27.0 62.6 %copy-start.22 = (s32[1026]{0:T(1024)}, s32[1026]{0:T(1024)S(1)}, u32[]{:S(2)}) copy-start(s32[1026]{0:T(1024)S(1)} %select_reduce_fusion) | copy-start | bytes 12316
  64.6 9.1 copy-start.7
  85.3 137.7 %all-to-all-start.1 = ((f32[128,8,256]{0,2,1:T(8,128)}), f32[128,8,256]{0,2,1:T(8,128)S(1)}, u32[]{:S(2)}, u32[]{:S(2)}) async-start(f32[128,8,256]{0,2,1:T(8,128)} %bitcast.273), calls=%async_computation.1 | async-start | bytes 2097152 | tf_op jit(solution)/shard_map/all_to_all | solution.py:236
  88.8 590.7 %all-gather.11.cloned.1.call-start = ((), (), s32[]{:S(2)}) async-start(), calls=%async_computation.4 | async-start | bytes 10649600 | tf_op jit(solution)/shard_map/all_gather | solution.py:15
  997.8 7.0 copy-start.1
  1004.9 14.0 %copy-start.14 = (f32[136,2,1024]{2,1,0:T(2,128)S(1)}, f32[136,2,1024]{2,1,0:T(2,128)}, u32[]{:S(2)}) copy-start(f32[136,2,1024]{2,1,0:T(2,128)} %get-tuple-element.1102) | copy-start | bytes 3342340
  1027.7 7.6 slice-start
  1027.7 7.6 copy-start.12
  1048.0 41.0 %copy-start.26 = (f32[128]{0:T(128)S(1)}, f32[128]{0:T(128)}, u32[]{:S(2)}) copy-start(f32[128]{0:T(128)} %copy-done.25) | copy-start | bytes 1540
  1048.1 41.0 %copy-start.28 = (f32[128]{0:T(128)S(1)}, f32[128]{0:T(128)}, u32[]{:S(2)}) copy-start(f32[128]{0:T(128)} %copy-done.27) | copy-start | bytes 1540
  1048.3 40.7 %copy-start.4 = (f32[128,2560]{0,1:T(8,128)S(1)}, f32[128,2560]{0,1:T(8,128)}, u32[]{:S(2)}) copy-start(f32[128,2560]{0,1:T(8,128)} %copy-done.3) | copy-start | bytes 3932164
  1048.3 40.7 %copy-start.6 = (f32[2,2560]{0,1:T(8,128)S(1)}, f32[2,2560]{0,1:T(8,128)}, u32[]{:S(2)}) copy-start(f32[2,2560]{0,1:T(8,128)} %copy-done.5) | copy-start | bytes 61444
  1091.3 99.4 %copy-start.17 = (f32[2560]{0:T(1024)S(1)}, f32[2560]{0:T(1024)}, u32[]{:S(2)}) copy-start(f32[2560]{0:T(1024)} %copy-done.16) | copy-start | bytes 30724
  1091.3 99.4 %copy-start.19 = (f32[2560]{0:T(1024)S(1)}, f32[2560]{0:T(1024)}, u32[]{:S(2)}) copy-start(f32[2560]{0:T(1024)} %copy-done.18) | copy-start | bytes 30724
  1091.3 99.4 %copy-start.21 = (f32[2560]{0:T(1024)S(1)}, f32[2560]{0:T(1024)}, u32[]{:S(2)}) copy-start(f32[2560]{0:T(1024)} %copy-done.20) | copy-start | bytes 30724
  1091.3 99.4 %copy-start.30 = (f32[128]{0:T(128)S(1)}, f32[128]{0:T(128)}, u32[]{:S(2)}) copy-start(f32[128]{0:T(128)} %get-tuple-element.1110) | copy-start | bytes 1540
  1091.3 99.4 %copy-start.31 = (f32[128]{0:T(128)S(1)}, f32[128]{0:T(128)}, u32[]{:S(2)}) copy-start(f32[128]{0:T(128)} %get-tuple-element.1112) | copy-start | bytes 1540
  1091.7 97.5 %collective-permute-start.1 = (f32[2,2560]{1,0:T(2,128)S(1)}, f32[2,2560]{1,0:T(2,128)S(1)}, u32[]{:S(2)}, u32[]{:S(2)}) collective-permute-start(f32[2,2560]{1,0:T(2,128)S(1)} %copy.144), channel_id=1, source_target_pairs={{1,0},{2,1},{3,2},{4,3},{5,4},{6,5},{7,6},{8,7},{9,8},{10,9},{11,1... | collective-permute-start | bytes 61448 | tf_op jit(solution)/shard_map/ppermute | solution.py:32
  (16 other events, 35.8 us)
Sparse Core Ops, SparseCore 0:
  84.0 91.8 all-gather.8
  590.8 88.6 all-gather.10
where the time goes:
time: 1220 us; the launch traced here: 1200 us
  other arithmetic  462 us (38%)
  blocking collectives  368 us (30%)
  local copies, waits for them, and re-layouts  129 us (11%)
  matrix products  118 us (10%)
  waiting for transfers between devices  69.8 us (6%)
  loops' own time  25.3 us (2%)
  starting transfers between devices  15.7 us (1%)
  between operations  15.7 us (1%)
    select_n x256, other arithmetic, lap(): return jax.tree.map(lambda a, b: jnp.where(reached, a, b), new, before)  301 us
    unnamed x1, blocking collectives  131 us
    all_gather x2, blocking collectives, carried_in(): everything = jax.tree.map(lambda part: lax.all_gather(part, axis), x)  101 us
    psum x1, blocking collectives, on_device(): grad_conv = lax.psum(weight_part, ('seq', 'head'))  95.5 us
    sub x128, other arithmetic, combine(): carry_keep = 1.0 - following[2]  78.9 us
    dynamic_update_slice x48, local copies, waits for them, and re-layouts, attention_grads(): forward_out = lax.scan(forward_block, (prefix[0], prefix[1]), indices)  55 us
    all_to_all x1, blocking collectives, on_device(): lax.all_to_all(grad_mixed, 'head', split_axis=0, concat_axis=1, tiled=True)  40.7 us
    all_gather x2, waiting for transfers between devices, carried_in(): everything = jax.tree.map(lambda part: lax.all_gather(part, axis), x)  36.5 us
  transfers between devices with their start and end apart: 6, of which 2 were waited for; matrix products, arithmetic and copies ran while one was open for 2% of the time, Pallas kernels for 0%

commit v1 on v0

--- a/solution.py
+++ b/solution.py
@@ -242,7 +242,7 @@
     grad_projected, weight_part = conv_backward(
         returned, trailing, projected, leading, conv_weight, token_offsets
     )
-    grad_conv = lax.psum(weight_part, ("seq", "head"))
+    grad_conv = jnp.sum(lax.all_gather(weight_part, ("seq", "head")), axis=0)
     return (grad_projected, grad_conv)
 
 

time: 1220 us -> 1250 us (1.025)
  waiting for transfers between devices: 69.8 us -> 193 us
  blocking collectives: 368 us -> 274 us
    all_gather x0 -> x1, waiting for transfers between devices: none -> 120 us  [on_device(): grad_conv = jnp.sum(lax.all_gather(weight_part, ('seq', 'head')), axis=0)]
    psum x1 -> x0, blocking collectives: 95.5 us -> none  [on_device(): grad_conv = lax.psum(weight_part, ('seq', 'head'))]
    reduce_sum x0 -> x1, other arithmetic: none -> 12.6 us  [on_device(): grad_conv = jnp.sum(lax.all_gather(weight_part, ('seq', 'head')), axis=0)]
  transfers between devices with their start and end apart: 6 -> 7, of which waited for: 2 -> 4; matrix products, arithmetic and copies ran while one was open for 2% -> 2% of each run, Pallas kernels for 0% -> 0%
where the time goes in v1:
time: 1250 us; the launch traced here: 1240 us
  other arithmetic  464 us (37%)
  blocking collectives  274 us (22%)
  waiting for transfers between devices  193 us (15%)
  local copies, waits for them, and re-layouts  135 us (11%)
  matrix products  118 us (9%)
  loops' own time  25.9 us (2%)
  starting transfers between devices  15.7 us (1%)
  between operations  15.3 us (1%)
    select_n x256, other arithmetic, lap(): return jax.tree.map(lambda a, b: jnp.where(reached, a, b), new, before)  294 us
    unnamed x1, blocking collectives  132 us
    all_gather x1, waiting for transfers between devices, on_device(): grad_conv = jnp.sum(lax.all_gather(weight_part, ('seq', 'head')), axis=0)  120 us
    all_gather x2, blocking collectives, carried_in(): everything = jax.tree.map(lambda part: lax.all_gather(part, axis), x)  101 us
    sub x128, other arithmetic, combine(): carry_keep = 1.0 - following[2]  75.4 us
    dynamic_update_slice x48, local copies, waits for them, and re-layouts, attention_grads(): forward_out = lax.scan(forward_block, (prefix[0], prefix[1]), indices)  54.8 us
    all_to_all x1, blocking collectives, on_device(): lax.all_to_all(grad_mixed, 'head', split_axis=0, concat_axis=1, tiled=True)  40.8 us
    all_gather x2, waiting for transfers between devices, carried_in(): everything = jax.tree.map(lambda part: lax.all_gather(part, axis), x)  36.4 us
  transfers between devices with their start and end apart: 7, of which 4 were waited for; matrix products, arithmetic and copies ran while one was open for 2% of the time, Pallas kernels for 0%

profile of v1, /device:TPU:1, one launch (start us, length us, event | category | flops | bytes accessed | tf_op | source)
XLA Modules:
  0.0 1240.6 jit_solution(9369790844008259987)
XLA Ops:
  20.1 6.1 all-to-all-start
  27.7 33.3 %all-to-all-done = f32[128,8,320]{0,2,1:T(8,128)S(1)} async-done(((f32[128,8,320]{0,2,1:T(8,128)}), f32[128,8,320]{0,2,1:T(8,128)S(1)}, u32[]{:S(2)}, u32[]{:S(2)}) %all-to-all-start) | async-done | bytes 1310752 | tf_op jit(solution)/shard_map/all_to_all | solution.py:235
  94.8 131.7 %all-reduce = f32[64]{0:T(128)S(1)} all-reduce(f32[64]{0:T(128)S(1)} %dynamic-update-slice), channel_id=1, replica_groups=mesh['seq'=64,'head'=8] {'seq'}, use_global_device_ids=true, to_apply=%add | all-reduce | flops 64 | bytes 512
  236.0 51.6 %all-gather.5 = f32[64,2,153]{2,1,0:T(2,128)S(1)} all-gather(f32[1,2,153]{2,1,0:T(2,128)S(1)} %copy.127), channel_id=3, replica_groups=mesh['seq'=64,'head'=8] {'seq'}, dimensions={0}, use_global_device_ids=true | all-gather | bytes 79560 | tf_op jit(solution)/shard_map/all_gather | solution.py:15
  287.6 187.7 %while.82 = (s32[]{:T(128)}, f32[2,153,128]{2,1,0:T(8,128)S(1)}, f32[2,153]{1,0:T(2,128)S(1)}, s32[]{:T(128)}, f32[64,2,153,128]{3,2,1,0:T(8,128)}, /*index=5*/f...) while((s32[]{:T(128)}, f32[2,153,128]{2,1,0:T(8,128)S(1)}, ...), condition=%wide.region_5.6_spmd.clone, body=%wide.region_4.5_spmd.clone.sunk | while | flops 157901 | bytes 473831 | solution.py:26
  476.6 110.1 %while.80 = (s32[]{:T(128)}, f32[2,153,128]{2,1,0:T(8,128)S(1)}, f32[2,153]{1,0:T(2,128)S(1)}, f32[8,128,2,128]{1,0,3,2:T(8,128)}, f32[8,2,128]{2,1,0:T(2,128)S(...) while((s32[]{:T(128)}, f32[2,153,128]{2,1,0:T(8,128)S(1)}, ...), condition=%wide.region_9.10_spmd.clone, body=%wide.region_6.9_spmd.clone.sunk | while | flops 231664960 | bytes 3280461 | solution.py:149
  480.6 4.7 dynamic_update_slice.74
  494.4 4.7 dynamic_update_slice.74
  508.2 4.7 dynamic_update_slice.74
  521.9 4.7 dynamic_update_slice.74
  535.7 4.7 dynamic_update_slice.74
  549.5 4.7 dynamic_update_slice.74
  597.1 49.5 %all-gather.6 = f32[64,2,153]{2,1,0:T(2,128)S(1)} all-gather(f32[1,2,153]{2,1,0:T(2,128)S(1)} %bitcast.284), channel_id=5, replica_groups=mesh['seq'=64,'head'=8] {'seq'}, dimensions={0}, use_global_device_ids=true | all-gather | bytes 79560 | tf_op jit(solution)/shard_map/all_gather | solution.py:15
  646.6 36.4 %all-gather.14.cloned.1.call-done = f32[128,153,128]{2,1,0:T(8,128)} async-done(((f32[2,153,128]{2,1,0:T(8,128)}), f32[128,153,128]{2,1,0:T(8,128)}) %all-gather.14.cloned.1.call-update) | async-done | bytes 10027024 | tf_op jit(solution)/shard_map/all_gather | solution.py:15
  683.0 184.7 %while.83 = (s32[]{:T(128)}, f32[2,153,128]{2,1,0:T(8,128)S(1)}, f32[2,153]{1,0:T(2,128)S(1)}, s32[]{:T(128)}, f32[64,2,153,128]{3,2,1,0:T(8,128)}, /*index=5*/f...) while((s32[]{:T(128)}, f32[2,153,128]{2,1,0:T(8,128)S(1)}, ...), condition=%wide.region_12.13_spmd.clone, body=%wide.region_11.12_spmd.clone.sunk | while | flops 157905 | bytes 473893 | solution.py:26
  871.2 113.0 %while.81 = (s32[]{:T(128)}, f32[2,153,128]{2,1,0:T(8,128)S(1)}, f32[2,153]{1,0:T(2,128)S(1)}, f32[8,2,153,128]{3,2,1,0:T(8,128)}, f32[8,2,153,128]{3,2,1,0:T(8,...) while((s32[]{:T(128)}, f32[2,153,128]{2,1,0:T(8,128)S(1)}, ...), condition=%wide.region_14.15_spmd.clone, body=%wide.region_13.14_spmd.clone.sunk | while | flops 462717824 | bytes 4866477 | solution.py:209
  992.7 5.9 fusion.90
  998.7 14.0 %scatter_fusion = f32[2,16,1024]{2,0,1:T(2,128)S(1)} fusion(f32[2,16,1024]{2,0,1:T(2,128)S(1)} %split.16, s32[136]{0:T(256)S(1)} %copy-done.16, f32[136,2,1024]{2,1,0:T(2,128)} %get-tuple-element.1103), kind=kCustom, calls=%fused_computation.4 | custom fusion | flops 278528 | bytes 3342880 | tf_op jit(solution)/shard_map/transpose(jvp())/scatter-add | solution.py:39
  1012.7 7.6 scatter_fusion.1
  1021.8 7.6 scatter_fusion.3
  1029.4 7.6 scatter_fusion.2
  1044.8 40.8 %all_to_all.51 = f32[8,128,320]{1,2,0:T(8,128)S(1)} all-to-all(f32[8,128,320]{1,2,0:T(8,128)S(1)} %copy.143), channel_id=1, replica_groups=mesh['seq'=64,'head'=8] {'head'}, dimensions={0} | all-to-all | bytes 2621440 | tf_op jit(solution)/shard_map/all_to_all | solution.py:240
  1100.8 120.5 %all-gather.16.cloned.1.call-done = f32[512,3,2560]{2,1,0:T(4,128)} async-done(((f32[1,3,2560]{2,1,0:T(4,128)}), f32[512,3,2560]{2,1,0:T(4,128)}) %all-gather.16.cloned.1.call-update) | async-done | bytes 15728656 | tf_op jit(solution)/shard_map/all_gather | solution.py:245
  1221.2 12.6 %reduce_sum.77 = f32[3,2560]{1,0:T(4,128)} reduce(f32[512,3,2560]{2,1,0:T(4,128)} %all-gather.16.cloned.1.call-done, f32[]{:T(128)} %constant.210.clone.1), dimensions={0}, to_apply=%region_22.23 | reduce | flops 3924480 | bytes 15759364 | tf_op jit(solution)/shard_map/reduce_sum | solution.py:245
  (815 shorter events, 646.1 us)
Async XLA Ops:
  8.1 8.5 collective-permute-start
  16.6 3.5 copy-start.3
  17.0 3.1 copy-start.5
  20.1 6.9 copy-start.17
  20.1 6.9 copy-start.16
  20.1 40.9 %all-to-all-start = ((f32[128,8,320]{0,2,1:T(8,128)}), f32[128,8,320]{0,2,1:T(8,128)S(1)}, u32[]{:S(2)}, u32[]{:S(2)}) async-start(f32[128,8,320]{0,2,1:T(8,128)} %bitcast.267), calls=%async_computation | async-start | bytes 2621440 | tf_op jit(solution)/shard_map/all_to_all | solution.py:235
  26.2 261.4 %all-gather.12.cloned.1.call-start = ((), (), s32[]{:S(2)}) async-start(), calls=%async_computation.3 | async-start | bytes 10649600 | tf_op jit(solution)/shard_map/all_gather | solution.py:15
  26.3 66.4 %copy-start.15 = (s32[1026]{0:T(1024)}, s32[1026]{0:T(1024)S(1)}, u32[]{:S(2)}) copy-start(s32[1026]{0:T(1024)S(1)} %select_reduce_fusion) | copy-start | bytes 12316
  73.9 3.1 copy-start.18
  84.7 2.3 copy-start.14
  88.4 138.1 %all-to-all-start.1 = ((f32[128,8,256]{0,2,1:T(8,128)}), f32[128,8,256]{0,2,1:T(8,128)S(1)}, u32[]{:S(2)}, u32[]{:S(2)}) async-start(f32[128,8,256]{0,2,1:T(8,128)} %bitcast.275), calls=%async_computation.1 | async-start | bytes 2097152 | tf_op jit(solution)/shard_map/all_to_all | solution.py:236
  91.9 591.0 %all-gather.14.cloned.1.call-start = ((), (), s32[]{:S(2)}) async-start(), calls=%async_computation.4 | async-start | bytes 10649600 | tf_op jit(solution)/shard_map/all_gather | solution.py:15
  230.5 1.7 copy-start.10
  589.0 2.9 copy-start.2
  594.2 627.0 %all-gather.16.cloned.1.call-start = ((), (), s32[]{:S(2)}) async-start(), calls=%async_computation.5 | async-start | bytes 21012480 | tf_op jit(solution)/shard_map/all_gather | solution.py:245
  986.2 1.7 copy-start.8
  989.7 3.1 copy-start.7
  991.6 7.0 copy-start.1
  998.6 14.0 %copy-start.13 = (f32[136,2,1024]{2,1,0:T(2,128)S(1)}, f32[136,2,1024]{2,1,0:T(2,128)}, u32[]{:S(2)}) copy-start(f32[136,2,1024]{2,1,0:T(2,128)} %get-tuple-element.1102) | copy-start | bytes 3342340
  1021.7 7.6 slice-start
  1021.7 7.6 copy-start.11
  1044.8 40.9 %copy-start.4 = (f32[128,2560]{0,1:T(8,128)S(1)}, f32[128,2560]{0,1:T(8,128)}, u32[]{:S(2)}) copy-start(f32[128,2560]{0,1:T(8,128)} %copy-done.3) | copy-start | bytes 3932164
  1044.8 40.8 %copy-start.6 = (f32[2,2560]{0,1:T(8,128)S(1)}, f32[2,2560]{0,1:T(8,128)}, u32[]{:S(2)}) copy-start(f32[2,2560]{0,1:T(8,128)} %copy-done.5) | copy-start | bytes 61444
  1088.9 4.5 collective-permute-start.1
  (4 other events, 5.0 us)
Sparse Core Ops, SparseCore 0:
  87.2 91.7 all-gather.11
  594.3 88.6 all-gather.13
  1088.6 132.5 all-gather.15
